TPU v7x, 256 devices: a whole 4x4x8 slice. The times are simulated.
256 devices in a mesh: space: 16 (over x_hi, z), chan: 8 (over y, core), dp: 2 (over x_lo).
Axes of the slice: x: 4 (x_hi: 2, x_lo: 2; x = x_hi * 2 + x_lo), y: 4, z: 8, core: 2. Of those that a mesh axis runs over, the one named last changes fastest.
Arguments:
- inputs: bfloat16 [2, 32, 8, 128, 512], P('dp', 'space', None, 'chan'), may hold values from -6 to 6
- cotangent: bfloat16 [2, 32, 8, 128, 512], P('dp', 'space', None, 'chan'), may hold values from -6 to 6
- weight: bfloat16 [27, 128, 128], P(None, 'chan'), may hold values from -0.109375 to 0.109375
Outputs:
- input_grad: bfloat16 [2, 32, 8, 128, 512], P('dp', 'space', None, 'chan')
- weight_grad: float32 [27, 128, 128], P(None, 'chan')
All inputs are finite; a program needn't handle non-finite values.
Results may differ from a plain program's by a relative error of at most 0.001.
Values may be sent and summed in bfloat16 or wider, within the bound.
No kernel may reach another device: no remote copies, remote signals or barrier semaphores. Data moves between devices by JAX's collectives and lax.ppermute only.
A program may use at most 64 MiB of HBM per device.

v0:
```python
import math
import jax
import jax.numpy as jnp
from jax import lax
from jax.sharding import PartitionSpec as P


def from_behind(value, axis, steps):
    count = lax.axis_size(axis)
    initial, last = (max(0, -steps), min(count, count - steps))
    return lax.ppermute(value, axis, [(source, source + steps) for source in range(initial, last)])


def exchange_sum(value, axis, distance):
    count = lax.axis_size(axis)
    return value + lax.ppermute(value, axis, [(i, i ^ distance) for i in range(count)])


def butterfly_sum(value):
    value = exchange_sum(value, "dp", 1)
    for distance in (1, 8, 2, 4):
        value = exchange_sum(value, "space", distance)
    return value


def shift_cells(block, step_z, step_y):
    zero = jnp.zeros((), block.dtype)
    config = ((0, 0, 0), (0, 0, 0), (step_z, -step_z, 0), (0, 0, 0), (step_y, -step_y, 0))
    return lax.pad(block, zero, config)


def local(inputs, cotangent, weight):
    samples, planes, depth, channels, width = inputs.shape
    outputs = weight.shape[2]
    inputs_ext = jnp.concatenate(
        [from_behind(inputs[:, -1:], "space", 1), inputs, from_behind(inputs[:, :1], "space", -1)],
        axis=1,
    )
    gathered = lax.all_gather(cotangent, "chan", axis=3, tiled=True)
    stacked = jnp.concatenate(
        [
            shift_cells(inputs_ext, -step_z, -step_y)
            for step_z in (-1, 0, 1)
            for step_y in (-1, 0, 1)
        ],
        axis=3,
    )
    groups = []
    for step_x in (-1, 0, 1):
        source = stacked[:, 1 + step_x : 1 + step_x + planes]
        groups.append(
            jnp.einsum("bxzky,bxzcy->kc", source, gathered, preferred_element_type=jnp.float32)
        )
    local_grad = jnp.concatenate(groups, axis=0).reshape(27, channels, outputs)
    count = samples * lax.axis_size("dp") * planes * lax.axis_size("space") * depth * width
    scale = 1.0 / math.sqrt(count)
    weight_grad = butterfly_sum(local_grad) * scale
    contrib = {}
    for step_x in (-1, 0, 1):
        first = 9 * (step_x + 1)
        total = None
        for step_y in (-1, 0, 1):
            kernel = weight[first + step_y + 1 : first + 9 : 3].reshape(3 * channels, outputs)
            product = jnp.einsum(
                "bxzcy,kc->bxzky", gathered, kernel, preferred_element_type=jnp.float32
            )
            for place, step_z in enumerate((-1, 0, 1)):
                part = shift_cells(
                    product[:, :, :, place * channels : (place + 1) * channels], step_z, step_y
                )
                total = part if total is None else total + part
        contrib[step_x] = total
    from_prev = from_behind(contrib[1][:, -1:], "space", 1)
    from_next = from_behind(contrib[-1][:, :1], "space", -1)
    accum = (
        contrib[0]
        + jnp.concatenate([from_prev, contrib[1][:, : planes - 1]], axis=1)
        + jnp.concatenate([contrib[-1][:, 1:], from_next], axis=1)
    )
    input_grad = accum.astype(jnp.bfloat16)
    return (input_grad, weight_grad)


def solution(mesh):
    placed = (
        P("dp", "space", None, "chan", None),
        P("dp", "space", None, "chan", None),
        P(None, "chan", None),
    )
    return jax.shard_map(
        local,
        mesh=mesh,
        in_specs=placed,
        out_specs=(P("dp", "space", None, "chan", None), P(None, "chan", None)),
        check_vma=False,
    )
```

profile of v0, /device:TPU:96, one launch (start us, length us, event | category | flops | bytes accessed | tf_op | source)
XLA Modules:
  0.0 112.7 jit_solution(3024075588676889384)
XLA Ops:
  8.9 5.0 %collective-permute-start.2 = (bf16[1,1,8,16,512]{4,3,2,1,0:T(8,128)(2,1)S(1)}, bf16[1,1,8,16,512]{4,3,2,1,0:T(8,128)(2,1)S(1)}, u32[]{:S(2)}, u32[]{:S(2)}) collective-permute-start(bf16[1,1,8,16,512]{4,3,2,1,0:T(8,128)(2,1)S(1)} %get-tuple-element.31), channel_id=1, source_target_pairs={{0,16},{16,32},{32,48},{48,64},{64,80},{80,96},{96,112},{112,128},... | collective-permute-start | bytes 393224 | tf_op jit(solution)/shard_map/ppermute | solution.py:11
  13.9 1.9 %collective-permute-start.3 = (bf16[1,1,8,16,512]{4,3,2,1,0:T(8,128)(2,1)S(1)}, bf16[1,1,8,16,512]{4,3,2,1,0:T(8,128)(2,1)S(1)}, u32[]{:S(2)}, u32[]{:S(2)}) collective-permute-start(bf16[1,1,8,16,512]{4,3,2,1,0:T(8,128)(2,1)S(1)} %get-tuple-element.30), channel_id=1, source_target_pairs={{16,0},{32,16},{48,32},{64,48},{80,64},{96,80},{112,96},{128,112},... | collective-permute-start | bytes 393224 | tf_op jit(solution)/shard_map/ppermute | solution.py:11
  17.7 4.3 %collective-permute-done.3 = bf16[1,1,8,16,512]{4,3,2,1,0:T(8,128)(2,1)S(1)} collective-permute-done((bf16[1,1,8,16,512]{4,3,2,1,0:T(8,128)(2,1)S(1)}, bf16[1,1,8,16,512]{4,3,2,1,0:T(8,128)(2,1)S(1)}, u32[]{:S(2)}, u32[]{:S(2)}) %collective-permute-start.3) | collective-permute-done | bytes 131104 | tf_op jit(solution)/shard_map/ppermute | solution.py:11
  22.0 1.0 fusion.91
  23.9 1.1 fusion.92
  25.0 1.2 %fusion.83 = bf16[1,4,8,144,512]{4,3,2,1,0:T(8,128)(2,1)} fusion(bf16[1,4,8,144,512]{4,3,2,1,0:T(8,128)(2,1)} %fusion.92, bf16[1,4,8,16,512]{4,3,2,1,0:T(8,128)(2,1)S(1)} %constant_dynamic-update-slice_fusion), kind=kLoop, calls=%fused_computation.94 | loop fusion | bytes 1048576
  28.3 1.1 %fusion.84 = bf16[1,4,8,144,512]{4,3,2,1,0:T(8,128)(2,1)} fusion(bf16[1,4,8,144,512]{4,3,2,1,0:T(8,128)(2,1)} %constant_dynamic-update-slice_fusion.3, bf16[1,4,8,16,512]{4,3,2,1,0:T(8,128)(2,1)S(1)} %constant_dynamic-update-slice_fusion), kind=kLoop, calls=%fused_computation.95 | loop fusion | bytes 1048576
  29.4 1.0 fusion.93
  31.4 1.1 fusion.94
  32.4 7.2 %all-gather.2.cloned.1.call-done = bf16[1,2,8,128,512]{4,3,2,1,0:T(8,128)(2,1)} async-done(((bf16[1,2,8,16,512]{4,3,2,1,0:T(8,128)(2,1)}), bf16[1,2,8,128,512]{4,3,2,1,0:T(8,128)(2,1)}) %all-gather.2.cloned.1.call-update) | async-done | bytes 2097168 | tf_op jit(solution)/shard_map/all_gather | solution.py:39
  39.6 3.2 %fusion.51 = f32[144,128]{1,0:T(8,128)S(1)} fusion(bf16[1,2,8,128,512]{4,3,2,1,0:T(8,128)(2,1)} %all-gather.2.cloned.1.call-done, bf16[1,4,8,144,512]{4,3,2,1,0:T(8,128)(2,1)} %fusion.94), kind=kOutput, calls=%fused_computation.36 | convolution fusion | flops 301989888 | bytes 4530176 | tf_op jit(solution)/shard_map/bxzky,bxzcy->kc/dot_general | solution.py:52
  42.8 2.4 %fusion.54 = f32[144,128]{1,0:T(8,128)S(1)} fusion(bf16[1,2,8,128,512]{4,3,2,1,0:T(8,128)(2,1)S(1)} %copy-done, bf16[1,4,8,144,512]{4,3,2,1,0:T(8,128)(2,1)} %fusion.94), kind=kOutput, calls=%fused_computation.37 | convolution fusion | flops 301989888 | bytes 4530176 | tf_op jit(solution)/shard_map/bxzky,bxzcy->kc/dot_general | solution.py:52
  45.3 2.4 %fusion.57 = f32[144,128]{1,0:T(8,128)S(1)} fusion(bf16[1,2,8,128,512]{4,3,2,1,0:T(8,128)(2,1)S(1)} %copy-done, bf16[1,4,8,144,512]{4,3,2,1,0:T(8,128)(2,1)} %fusion.94), kind=kOutput, calls=%fused_computation.38 | convolution fusion | flops 301989888 | bytes 4530176 | tf_op jit(solution)/shard_map/bxzky,bxzcy->kc/dot_general | solution.py:52
  47.7 1.6 %collective-permute-start.4 = (f32[27,16,128]{2,1,0:T(8,128)S(1)}, f32[27,16,128]{2,1,0:T(8,128)S(1)}, u32[]{:S(2)}, u32[]{:S(2)}) collective-permute-start(f32[27,16,128]{2,1,0:T(8,128)S(1)} %bitcast.167), channel_id=1, source_target_pairs={{0,1},{1,0},{2,3},{3,2},{4,5},{5,4},{6,7},{7,6},{8,9},{9,8},{10,11... | collective-permute-start | bytes 663560 | tf_op jit(solution)/shard_map/ppermute | solution.py:16
  52.1 2.4 %collective-permute-start.1 = (f32[1,1,8,16,512]{4,3,2,1,0:T(8,128)S(1)}, f32[1,1,8,16,512]{4,3,2,1,0:T(8,128)S(1)}, u32[]{:S(2)}, u32[]{:S(2)}) collective-permute-start(f32[1,1,8,16,512]{4,3,2,1,0:T(8,128)S(1)} %get-tuple-element.27), channel_id=1, source_target_pairs={{16,0},{32,16},{48,32},{64,48},{80,64},{96,80},{112,96},{128,112},... | collective-permute-start | bytes 786440 | tf_op jit(solution)/shard_map/ppermute | solution.py:11
  57.3 4.7 %collective-permute-start = (f32[1,1,8,16,512]{4,3,2,1,0:T(8,128)S(1)}, f32[1,1,8,16,512]{4,3,2,1,0:T(8,128)S(1)}, u32[]{:S(2)}, u32[]{:S(2)}) collective-permute-start(f32[1,1,8,16,512]{4,3,2,1,0:T(8,128)S(1)} %get-tuple-element.28), channel_id=1, source_target_pairs={{0,16},{16,32},{32,48},{48,64},{64,80},{80,96},{96,112},{112,128},... | collective-permute-start | bytes 786440 | tf_op jit(solution)/shard_map/ppermute | solution.py:11
  63.0 8.8 %collective-permute-done.5 = f32[27,16,128]{2,1,0:T(8,128)S(1)} collective-permute-done((f32[27,16,128]{2,1,0:T(8,128)S(1)}, f32[27,16,128]{2,1,0:T(8,128)S(1)}, u32[]{:S(2)}, u32[]{:S(2)}) %collective-permute-start.5) | collective-permute-done | bytes 221216 | tf_op jit(solution)/shard_map/ppermute | solution.py:16
  71.9 2.8 %collective-permute-start.6 = (f32[27,16,128]{2,1,0:T(8,128)S(1)}, f32[27,16,128]{2,1,0:T(8,128)S(1)}, u32[]{:S(2)}, u32[]{:S(2)}) collective-permute-start(f32[27,16,128]{2,1,0:T(8,128)S(1)} %add.184), channel_id=1, source_target_pairs={{0,128},{16,144},{32,160},{48,176},{64,192},{80,208},{96,224},{112... | collective-permute-start | bytes 663560 | tf_op jit(solution)/shard_map/ppermute | solution.py:16
  75.6 4.0 %collective-permute-done.6 = f32[27,16,128]{2,1,0:T(8,128)S(1)} collective-permute-done((f32[27,16,128]{2,1,0:T(8,128)S(1)}, f32[27,16,128]{2,1,0:T(8,128)S(1)}, u32[]{:S(2)}, u32[]{:S(2)}) %collective-permute-start.6) | collective-permute-done | bytes 221216 | tf_op jit(solution)/shard_map/ppermute | solution.py:16
  79.6 2.0 %collective-permute-start.7 = (f32[27,16,128]{2,1,0:T(8,128)S(1)}, f32[27,16,128]{2,1,0:T(8,128)S(1)}, u32[]{:S(2)}, u32[]{:S(2)}) collective-permute-start(f32[27,16,128]{2,1,0:T(8,128)S(1)} %add.185), channel_id=1, source_target_pairs={{0,32},{16,48},{32,0},{48,16},{64,96},{80,112},{96,64},{112,80},{1... | collective-permute-start | bytes 663560 | tf_op jit(solution)/shard_map/ppermute | solution.py:16
  81.8 7.9 %collective-permute-done.7 = f32[27,16,128]{2,1,0:T(8,128)S(1)} collective-permute-done((f32[27,16,128]{2,1,0:T(8,128)S(1)}, f32[27,16,128]{2,1,0:T(8,128)S(1)}, u32[]{:S(2)}, u32[]{:S(2)}) %collective-permute-start.7) | collective-permute-done | bytes 221216 | tf_op jit(solution)/shard_map/ppermute | solution.py:16
  89.7 3.9 %collective-permute-start.8 = (f32[27,16,128]{2,1,0:T(8,128)S(1)}, f32[27,16,128]{2,1,0:T(8,128)S(1)}, u32[]{:S(2)}, u32[]{:S(2)}) collective-permute-start(f32[27,16,128]{2,1,0:T(8,128)S(1)} %add.186), channel_id=1, source_target_pairs={{0,64},{16,80},{32,96},{48,112},{64,0},{80,16},{96,32},{112,48},{1... | collective-permute-start | bytes 663560 | tf_op jit(solution)/shard_map/ppermute | solution.py:16
  93.7 1.5 %fusion.70 = bf16[1,2,8,16,512]{4,3,2,1,0:T(8,128)(2,1)} fusion(f32[1,2,8,16,512]{4,3,2,1,0:T(8,128)S(1)} %get-tuple-element.25, f32[1,2,8,16,512]{4,3,2,1,0:T(8,128)S(1)} %get-tuple-element.24, f32[1,2,8,16,512]{4,3,2,1,0:T(8,128)S(1)} %get-tuple-element.48, f32[1,2,8,16,512]{4,3,2,1,0:T(8,128)S(1)} %get-tuple-element.19, ...), kind=kLoop, calls=%fused_computation.81 | loop fusion | flops 1703936 | bytes 6029312 | tf_op jit(solution)/shard_map/convert_element_type | solution.py:80
  95.2 9.9 %collective-permute-done.8 = f32[27,16,128]{2,1,0:T(8,128)S(1)} collective-permute-done((f32[27,16,128]{2,1,0:T(8,128)S(1)}, f32[27,16,128]{2,1,0:T(8,128)S(1)}, u32[]{:S(2)}, u32[]{:S(2)}) %collective-permute-start.8) | collective-permute-done | bytes 221216 | tf_op jit(solution)/shard_map/ppermute | solution.py:16
  (46 shorter events, 15.9 us)
Async XLA Ops:
  7.2 32.4 %all-gather.2.cloned.1.call-start = ((), (), s32[]{:S(2)}) async-start(), calls=%async_computation | async-start | bytes 2359296 | tf_op jit(solution)/shard_map/all_gather | solution.py:39
  8.9 7.8 %collective-permute-start.2 = (bf16[1,1,8,16,512]{4,3,2,1,0:T(8,128)(2,1)S(1)}, bf16[1,1,8,16,512]{4,3,2,1,0:T(8,128)(2,1)S(1)}, u32[]{:S(2)}, u32[]{:S(2)}) collective-permute-start(bf16[1,1,8,16,512]{4,3,2,1,0:T(8,128)(2,1)S(1)} %get-tuple-element.31), channel_id=1, source_target_pairs={{0,16},{16,32},{32,48},{48,64},{64,80},{80,96},{96,112},{112,128},... | collective-permute-start | bytes 393224 | tf_op jit(solution)/shard_map/ppermute | solution.py:11
  13.9 8.1 %collective-permute-start.3 = (bf16[1,1,8,16,512]{4,3,2,1,0:T(8,128)(2,1)S(1)}, bf16[1,1,8,16,512]{4,3,2,1,0:T(8,128)(2,1)S(1)}, u32[]{:S(2)}, u32[]{:S(2)}) collective-permute-start(bf16[1,1,8,16,512]{4,3,2,1,0:T(8,128)(2,1)S(1)} %get-tuple-element.30), channel_id=1, source_target_pairs={{16,0},{32,16},{48,32},{64,48},{80,64},{96,80},{112,96},{128,112},... | collective-permute-start | bytes 393224 | tf_op jit(solution)/shard_map/ppermute | solution.py:11
  22.0 4.8 %copy-start.1 = (bf16[1,2,8,16,512]{4,3,2,1,0:T(8,128)(2,1)S(1)}, bf16[1,2,8,16,512]{4,3,2,1,0:T(8,128)(2,1)}, u32[]{:S(2)}) copy-start(bf16[1,2,8,16,512]{4,3,2,1,0:T(8,128)(2,1)} %param.3) | copy-start | bytes 786436
  39.6 3.2 %copy-start = (bf16[1,2,8,128,512]{4,3,2,1,0:T(8,128)(2,1)S(1)}, bf16[1,2,8,128,512]{4,3,2,1,0:T(8,128)(2,1)}, u32[]{:S(2)}) copy-start(bf16[1,2,8,128,512]{4,3,2,1,0:T(8,128)(2,1)} %all-gather.2.cloned.1.call-done) | copy-start | bytes 6291460
  47.7 14.3 %collective-permute-start.4 = (f32[27,16,128]{2,1,0:T(8,128)S(1)}, f32[27,16,128]{2,1,0:T(8,128)S(1)}, u32[]{:S(2)}, u32[]{:S(2)}) collective-permute-start(f32[27,16,128]{2,1,0:T(8,128)S(1)} %bitcast.167), channel_id=1, source_target_pairs={{0,1},{1,0},{2,3},{3,2},{4,5},{5,4},{6,7},{7,6},{8,9},{9,8},{10,11... | collective-permute-start | bytes 663560 | tf_op jit(solution)/shard_map/ppermute | solution.py:16
  52.1 41.6 %collective-permute-start.1 = (f32[1,1,8,16,512]{4,3,2,1,0:T(8,128)S(1)}, f32[1,1,8,16,512]{4,3,2,1,0:T(8,128)S(1)}, u32[]{:S(2)}, u32[]{:S(2)}) collective-permute-start(f32[1,1,8,16,512]{4,3,2,1,0:T(8,128)S(1)} %get-tuple-element.27), channel_id=1, source_target_pairs={{16,0},{32,16},{48,32},{64,48},{80,64},{96,80},{112,96},{128,112},... | collective-permute-start | bytes 786440 | tf_op jit(solution)/shard_map/ppermute | solution.py:11
  57.3 36.4 %collective-permute-start = (f32[1,1,8,16,512]{4,3,2,1,0:T(8,128)S(1)}, f32[1,1,8,16,512]{4,3,2,1,0:T(8,128)S(1)}, u32[]{:S(2)}, u32[]{:S(2)}) collective-permute-start(f32[1,1,8,16,512]{4,3,2,1,0:T(8,128)S(1)} %get-tuple-element.28), channel_id=1, source_target_pairs={{0,16},{16,32},{32,48},{48,64},{64,80},{80,96},{96,112},{112,128},... | collective-permute-start | bytes 786440 | tf_op jit(solution)/shard_map/ppermute | solution.py:11
  62.0 9.8 %collective-permute-start.5 = (f32[27,16,128]{2,1,0:T(8,128)S(1)}, f32[27,16,128]{2,1,0:T(8,128)S(1)}, u32[]{:S(2)}, u32[]{:S(2)}) collective-permute-start(f32[27,16,128]{2,1,0:T(8,128)S(1)} %add.183), channel_id=1, source_target_pairs={{0,16},{16,0},{32,48},{48,32},{64,80},{80,64},{96,112},{112,96},{1... | collective-permute-start | bytes 663560 | tf_op jit(solution)/shard_map/ppermute | solution.py:16
  71.9 7.7 %collective-permute-start.6 = (f32[27,16,128]{2,1,0:T(8,128)S(1)}, f32[27,16,128]{2,1,0:T(8,128)S(1)}, u32[]{:S(2)}, u32[]{:S(2)}) collective-permute-start(f32[27,16,128]{2,1,0:T(8,128)S(1)} %add.184), channel_id=1, source_target_pairs={{0,128},{16,144},{32,160},{48,176},{64,192},{80,208},{96,224},{112... | collective-permute-start | bytes 663560 | tf_op jit(solution)/shard_map/ppermute | solution.py:16
  79.6 10.1 %collective-permute-start.7 = (f32[27,16,128]{2,1,0:T(8,128)S(1)}, f32[27,16,128]{2,1,0:T(8,128)S(1)}, u32[]{:S(2)}, u32[]{:S(2)}) collective-permute-start(f32[27,16,128]{2,1,0:T(8,128)S(1)} %add.185), channel_id=1, source_target_pairs={{0,32},{16,48},{32,0},{48,16},{64,96},{80,112},{96,64},{112,80},{1... | collective-permute-start | bytes 663560 | tf_op jit(solution)/shard_map/ppermute | solution.py:16
  89.7 15.4 %collective-permute-start.8 = (f32[27,16,128]{2,1,0:T(8,128)S(1)}, f32[27,16,128]{2,1,0:T(8,128)S(1)}, u32[]{:S(2)}, u32[]{:S(2)}) collective-permute-start(f32[27,16,128]{2,1,0:T(8,128)S(1)} %add.186), channel_id=1, source_target_pairs={{0,64},{16,80},{32,96},{48,112},{64,0},{80,16},{96,32},{112,48},{1... | collective-permute-start | bytes 663560 | tf_op jit(solution)/shard_map/ppermute | solution.py:16
Sparse Core Ops, SparseCore 0:
  9.8 29.7 all-gather.1
where the time goes:
time: 113 us
  waiting for transfers between devices  42.8 us (38%)
  starting transfers between devices  24.4 us (22%)
  local copies, waits for them, and re-layouts  15.3 us (14%)
  between operations  14.3 us (13%)
  matrix products  11.9 us (11%)
  other arithmetic  4 us (4%)
    ppermute x5, waiting for transfers between devices, exchange_sum(): lax.ppermute(value, axis, [(i, i ^ distance) for i in range(count)])  30.7 us
    ppermute x4, starting transfers between devices, from_behind(): lax.ppermute(value, axis, [(source, source + steps) for source in range(i...  14 us
    ppermute x5, starting transfers between devices, exchange_sum(): lax.ppermute(value, axis, [(i, i ^ distance) for i in range(count)])  10.4 us
    unnamed x16, local copies, waits for them, and re-layouts  10.3 us
    dot_general x3, matrix products, local(): jnp.einsum('bxzky,bxzcy->kc', source, gathered, preferred_element_type=jn...  8.07 us
    all_gather x1, waiting for transfers between devices, local(): gathered = lax.all_gather(cotangent, 'chan', axis=3, tiled=True)  7.18 us
    ppermute x4, waiting for transfers between devices, from_behind(): lax.ppermute(value, axis, [(source, source + steps) for source in range(i...  4.29 us
    dot_general x9, matrix products, local(): jnp.einsum('bxzcy,kc->bxzky', gathered, kernel, preferred_element_type=jn...  3.81 us
  transfers between devices with their start and end apart: 10, of which 6 were waited for; matrix products, arithmetic and copies ran while one was open for 20% of the time, Pallas kernels for 0%

commit v1 on v0

--- a/solution.py
+++ b/solution.py
@@ -1,8 +1,32 @@
+import functools
 import math
 import jax
 import jax.numpy as jnp
 from jax import lax
 from jax.sharding import PartitionSpec as P
+from jax.lax import axis_index, axis_size, ppermute
+
+
+def _wrap_records(local_values, mesh_dim):
+    wide_n = axis_size(mesh_dim)
+    rack = []
+    for idx in tuple(range(wide_n)):
+        rack.append((idx, (idx + 1) % wide_n))
+    arrivals = []
+    for idx in tuple(range(wide_n)):
+        arrivals.append((idx, (idx - 1) % wide_n))
+    earlier, mixed_arr = ([local_values], [local_values])
+    for _ in range(wide_n // 2):
+        earlier.append(ppermute(earlier[-1], mesh_dim, rack))
+    for _ in [*range((wide_n - 1) // 2)]:
+        tile_out = ppermute(mixed_arr[-1], mesh_dim, arrivals)
+        mixed_arr.append(tile_out)
+    r1 = jnp.concatenate([*earlier[::-1], *mixed_arr[1:]], 3)
+    raw_out = jnp.roll(r1, (axis_index(mesh_dim) - wide_n // 2) * local_values.shape[3], 3)
+    return raw_out
+
+
+lots_all_solve = functools.partial(_wrap_records, mesh_dim="chan")
 
 
 def from_behind(value, axis, steps):
@@ -36,7 +60,7 @@
         [from_behind(inputs[:, -1:], "space", 1), inputs, from_behind(inputs[:, :1], "space", -1)],
         axis=1,
     )
-    gathered = lax.all_gather(cotangent, "chan", axis=3, tiled=True)
+    gathered = lots_all_solve(cotangent)
     stacked = jnp.concatenate(
         [
             shift_cells(inputs_ext, -step_z, -step_y)

time: 113 us -> 102 us (0.903)
  the two profiles are of different devices: /device:TPU:96 before, /device:TPU:8 now
where the time goes in v1:
time: 102 us; the launch traced here: 101 us
  waiting for transfers between devices  51.1 us (50%)
  starting transfers between devices  32 us (31%)
  local copies, waits for them, and re-layouts  6.89 us (7%)
  matrix products  6.1 us (6%)
  other arithmetic  3.99 us (4%)
  between operations  1.11 us (1%)
    ppermute x5, waiting for transfers between devices, exchange_sum(): lax.ppermute(value, axis, [(i, i ^ distance) for i in range(count)])  34.6 us
    ppermute x5, starting transfers between devices, exchange_sum(): lax.ppermute(value, axis, [(i, i ^ distance) for i in range(count)])  15.6 us
    ppermute x4, waiting for transfers between devices, _wrap_records(): earlier.append(ppermute(earlier[-1], mesh_dim, rack))  12.2 us
    ppermute x4, starting transfers between devices, from_behind(): lax.ppermute(value, axis, [(source, source + steps) for source in range(i...  11 us
    ppermute x3, starting transfers between devices, _wrap_records(): tile_out = ppermute(mixed_arr[-1], mesh_dim, arrivals)  5.37 us
    ppermute x4, waiting for transfers between devices, from_behind(): lax.ppermute(value, axis, [(source, source + steps) for source in range(i...  3.98 us
    dot_general x9, matrix products, local(): jnp.einsum('bxzcy,kc->bxzky', gathered, kernel, preferred_element_type=jn...  3.79 us
    unnamed x31, local copies, waits for them, and re-layouts  2.69 us
  transfers between devices with their start and end apart: 16, of which 10 were waited for; matrix products, arithmetic and copies ran while one was open for 14% of the time, Pallas kernels for 0%

profile of v1, /device:TPU:8, one launch (start us, length us, event | category | flops | bytes accessed | tf_op | source)
XLA Modules:
  0.0 101.2 jit_solution(11319920972530246695)
XLA Ops:
  0.7 1.7 %collective-permute-start.4 = (bf16[1,2,8,16,512]{4,3,2,1,0:T(8,128)(2,1)}, bf16[1,2,8,16,512]{4,3,2,1,0:T(8,128)(2,1)S(1)}, u32[]{:S(2)}, u32[]{:S(2)}) collective-permute-start(bf16[1,2,8,16,512]{4,3,2,1,0:T(8,128)(2,1)} %param.4), channel_id=1, source_target_pairs={{0,14},{2,0},{4,2},{6,4},{8,6},{10,8},{12,10},{14,12},{1,15},{3,1}... | collective-permute-start | bytes 786440 | tf_op jit(solution)/shard_map/ppermute | solution.py:22
  2.4 1.0 fusion.106
  3.4 3.8 %collective-permute-start.9 = (bf16[1,1,8,16,512]{4,3,2,1,0:T(8,128)(2,1)S(1)}, bf16[1,1,8,16,512]{4,3,2,1,0:T(8,128)(2,1)S(1)}, u32[]{:S(2)}, u32[]{:S(2)}) collective-permute-start(bf16[1,1,8,16,512]{4,3,2,1,0:T(8,128)(2,1)S(1)} %get-tuple-element.31), channel_id=1, source_target_pairs={{0,16},{16,32},{32,48},{48,64},{64,80},{80,96},{96,112},{112,128},... | collective-permute-start | bytes 393224 | tf_op jit(solution)/shard_map/ppermute | solution.py:35
  7.2 1.3 %collective-permute-start.10 = (bf16[1,1,8,16,512]{4,3,2,1,0:T(8,128)(2,1)S(1)}, bf16[1,1,8,16,512]{4,3,2,1,0:T(8,128)(2,1)S(1)}, u32[]{:S(2)}, u32[]{:S(2)}) collective-permute-start(bf16[1,1,8,16,512]{4,3,2,1,0:T(8,128)(2,1)S(1)} %get-tuple-element.30), channel_id=1, source_target_pairs={{16,0},{32,16},{48,32},{64,48},{80,64},{96,80},{112,96},{128,112},... | collective-permute-start | bytes 393224 | tf_op jit(solution)/shard_map/ppermute | solution.py:35
  8.5 0.9 fusion.107
  10.1 1.0 constant_dynamic-update-slice_fusion.17
  11.1 3.3 %collective-permute-done.10 = bf16[1,1,8,16,512]{4,3,2,1,0:T(8,128)(2,1)S(1)} collective-permute-done((bf16[1,1,8,16,512]{4,3,2,1,0:T(8,128)(2,1)S(1)}, bf16[1,1,8,16,512]{4,3,2,1,0:T(8,128)(2,1)S(1)}, u32[]{:S(2)}, u32[]{:S(2)}) %collective-permute-start.10) | collective-permute-done | bytes 131104 | tf_op jit(solution)/shard_map/ppermute | solution.py:35
  15.3 5.2 %collective-permute-done.1 = bf16[1,2,8,16,512]{4,3,2,1,0:T(8,128)(2,1)S(1)} collective-permute-done((bf16[1,2,8,16,512]{4,3,2,1,0:T(8,128)(2,1)S(1)}, bf16[1,2,8,16,512]{4,3,2,1,0:T(8,128)(2,1)S(1)}, u32[]{:S(2)}, u32[]{:S(2)}) %collective-permute-start.1) | collective-permute-done | bytes 262176 | tf_op jit(solution)/shard_map/ppermute | solution.py:20
  20.8 1.8 %collective-permute-start.5 = (bf16[1,2,8,16,512]{4,3,2,1,0:T(8,128)(2,1)S(1)}, bf16[1,2,8,16,512]{4,3,2,1,0:T(8,128)(2,1)S(1)}, u32[]{:S(2)}, u32[]{:S(2)}) collective-permute-start(bf16[1,2,8,16,512]{4,3,2,1,0:T(8,128)(2,1)S(1)} %collective-permute-done.4), channel_id=1, source_target_pairs={{0,14},{2,0},{4,2},{6,4},{8,6},{10,8},{12,10},{14,12},{1,15},{3,1}... | collective-permute-start | bytes 786440 | tf_op jit(solution)/shard_map/ppermute | solution.py:22
  22.6 3.7 %collective-permute-done.2 = bf16[1,2,8,16,512]{4,3,2,1,0:T(8,128)(2,1)S(1)} collective-permute-done((bf16[1,2,8,16,512]{4,3,2,1,0:T(8,128)(2,1)S(1)}, bf16[1,2,8,16,512]{4,3,2,1,0:T(8,128)(2,1)S(1)}, u32[]{:S(2)}, u32[]{:S(2)}) %collective-permute-start.2) | collective-permute-done | bytes 262176 | tf_op jit(solution)/shard_map/ppermute | solution.py:20
  26.8 1.9 %collective-permute-start.6 = (bf16[1,2,8,16,512]{4,3,2,1,0:T(8,128)(2,1)S(1)}, bf16[1,2,8,16,512]{4,3,2,1,0:T(8,128)(2,1)S(1)}, u32[]{:S(2)}, u32[]{:S(2)}) collective-permute-start(bf16[1,2,8,16,512]{4,3,2,1,0:T(8,128)(2,1)S(1)} %collective-permute-done.5), channel_id=1, source_target_pairs={{0,14},{2,0},{4,2},{6,4},{8,6},{10,8},{12,10},{14,12},{1,15},{3,1}... | collective-permute-start | bytes 786440 | tf_op jit(solution)/shard_map/ppermute | solution.py:22
  28.7 3.4 %collective-permute-done.3 = bf16[1,2,8,16,512]{4,3,2,1,0:T(8,128)(2,1)S(1)} collective-permute-done((bf16[1,2,8,16,512]{4,3,2,1,0:T(8,128)(2,1)S(1)}, bf16[1,2,8,16,512]{4,3,2,1,0:T(8,128)(2,1)S(1)}, u32[]{:S(2)}, u32[]{:S(2)}) %collective-permute-start.3) | collective-permute-done | bytes 262176 | tf_op jit(solution)/shard_map/ppermute | solution.py:20
  35.2 1.6 %collective-permute-start.11 = (f32[27,16,128]{2,1,0:T(8,128)S(1)}, f32[27,16,128]{2,1,0:T(8,128)S(1)}, u32[]{:S(2)}, u32[]{:S(2)}) collective-permute-start(f32[27,16,128]{2,1,0:T(8,128)S(1)} %bitcast.185), channel_id=1, source_target_pairs={{0,1},{1,0},{2,3},{3,2},{4,5},{5,4},{6,7},{7,6},{8,9},{9,8},{10,11... | collective-permute-start | bytes 663560 | tf_op jit(solution)/shard_map/ppermute | solution.py:40
  38.7 0.8 fusion.82
  39.6 1.3 %collective-permute-start.8 = (f32[1,1,8,16,512]{4,3,2,1,0:T(8,128)S(1)}, f32[1,1,8,16,512]{4,3,2,1,0:T(8,128)S(1)}, u32[]{:S(2)}, u32[]{:S(2)}) collective-permute-start(f32[1,1,8,16,512]{4,3,2,1,0:T(8,128)S(1)} %get-tuple-element.27), channel_id=1, source_target_pairs={{16,0},{32,16},{48,32},{64,48},{80,64},{96,80},{112,96},{128,112},... | collective-permute-start | bytes 786440 | tf_op jit(solution)/shard_map/ppermute | solution.py:35
  43.7 4.6 %collective-permute-start.7 = (f32[1,1,8,16,512]{4,3,2,1,0:T(8,128)S(1)}, f32[1,1,8,16,512]{4,3,2,1,0:T(8,128)S(1)}, u32[]{:S(2)}, u32[]{:S(2)}) collective-permute-start(f32[1,1,8,16,512]{4,3,2,1,0:T(8,128)S(1)} %get-tuple-element.28), channel_id=1, source_target_pairs={{0,16},{16,32},{32,48},{48,64},{64,80},{80,96},{96,112},{112,128},... | collective-permute-start | bytes 786440 | tf_op jit(solution)/shard_map/ppermute | solution.py:35
  48.3 3.1 %collective-permute-start.12 = (f32[27,16,128]{2,1,0:T(8,128)S(1)}, f32[27,16,128]{2,1,0:T(8,128)S(1)}, u32[]{:S(2)}, u32[]{:S(2)}) collective-permute-start(f32[27,16,128]{2,1,0:T(8,128)S(1)} %add.196), channel_id=1, source_target_pairs={{0,16},{16,0},{32,48},{48,32},{64,80},{80,64},{96,112},{112,96},{1... | collective-permute-start | bytes 663560 | tf_op jit(solution)/shard_map/ppermute | solution.py:40
  52.3 7.3 %collective-permute-done.12 = f32[27,16,128]{2,1,0:T(8,128)S(1)} collective-permute-done((f32[27,16,128]{2,1,0:T(8,128)S(1)}, f32[27,16,128]{2,1,0:T(8,128)S(1)}, u32[]{:S(2)}, u32[]{:S(2)}) %collective-permute-start.12) | collective-permute-done | bytes 221216 | tf_op jit(solution)/shard_map/ppermute | solution.py:40
  59.6 8.6 %collective-permute-start.13 = (f32[27,16,128]{2,1,0:T(8,128)S(1)}, f32[27,16,128]{2,1,0:T(8,128)S(1)}, u32[]{:S(2)}, u32[]{:S(2)}) collective-permute-start(f32[27,16,128]{2,1,0:T(8,128)S(1)} %add.197), channel_id=1, source_target_pairs={{0,128},{16,144},{32,160},{48,176},{64,192},{80,208},{96,224},{112... | collective-permute-start | bytes 663560 | tf_op jit(solution)/shard_map/ppermute | solution.py:40
  69.2 4.9 %collective-permute-done.13 = f32[27,16,128]{2,1,0:T(8,128)S(1)} collective-permute-done((f32[27,16,128]{2,1,0:T(8,128)S(1)}, f32[27,16,128]{2,1,0:T(8,128)S(1)}, u32[]{:S(2)}, u32[]{:S(2)}) %collective-permute-start.13) | collective-permute-done | bytes 221216 | tf_op jit(solution)/shard_map/ppermute | solution.py:40
  74.4 12.5 %collective-permute-done.14 = f32[27,16,128]{2,1,0:T(8,128)S(1)} collective-permute-done((f32[27,16,128]{2,1,0:T(8,128)S(1)}, f32[27,16,128]{2,1,0:T(8,128)S(1)}, u32[]{:S(2)}, u32[]{:S(2)}) %collective-permute-start.14) | collective-permute-done | bytes 221216 | tf_op jit(solution)/shard_map/ppermute | solution.py:40
  87.0 2.2 %collective-permute-start.15 = (f32[27,16,128]{2,1,0:T(8,128)S(1)}, f32[27,16,128]{2,1,0:T(8,128)S(1)}, u32[]{:S(2)}, u32[]{:S(2)}) collective-permute-start(f32[27,16,128]{2,1,0:T(8,128)S(1)} %add.199), channel_id=1, source_target_pairs={{0,64},{16,80},{32,96},{48,112},{64,0},{80,16},{96,32},{112,48},{1... | collective-permute-start | bytes 663560 | tf_op jit(solution)/shard_map/ppermute | solution.py:40
  89.1 1.5 %fusion.70 = bf16[1,2,8,16,512]{4,3,2,1,0:T(8,128)(2,1)} fusion(f32[1,2,8,16,512]{4,3,2,1,0:T(8,128)S(1)} %get-tuple-element.25, f32[1,2,8,16,512]{4,3,2,1,0:T(8,128)S(1)} %get-tuple-element.24, f32[1,2,8,16,512]{4,3,2,1,0:T(8,128)S(1)} %get-tuple-element.48, f32[1,2,8,16,512]{4,3,2,1,0:T(8,128)S(1)} %get-tuple-element.19, ...), kind=kLoop, calls=%fused_computation.81 | loop fusion | flops 1703936 | bytes 6029312 | tf_op jit(solution)/shard_map/convert_element_type | solution.py:104
  90.6 9.9 %collective-permute-done.15 = f32[27,16,128]{2,1,0:T(8,128)S(1)} collective-permute-done((f32[27,16,128]{2,1,0:T(8,128)S(1)}, f32[27,16,128]{2,1,0:T(8,128)S(1)}, u32[]{:S(2)}, u32[]{:S(2)}) %collective-permute-start.15) | collective-permute-done | bytes 221216 | tf_op jit(solution)/shard_map/ppermute | solution.py:40
  (73 shorter events, 13.0 us)
Async XLA Ops:
  0.6 19.8 %copy-start = (bf16[1,2,8,16,512]{4,3,2,1,0:T(8,128)(2,1)S(1)}, bf16[1,2,8,16,512]{4,3,2,1,0:T(8,128)(2,1)}, u32[]{:S(2)}) copy-start(bf16[1,2,8,16,512]{4,3,2,1,0:T(8,128)(2,1)} %param.3) | copy-start | bytes 786436
  0.6 14.0 %collective-permute-start = (bf16[1,2,8,16,512]{4,3,2,1,0:T(8,128)(2,1)}, bf16[1,2,8,16,512]{4,3,2,1,0:T(8,128)(2,1)S(1)}, u32[]{:S(2)}, u32[]{:S(2)}) collective-permute-start(bf16[1,2,8,16,512]{4,3,2,1,0:T(8,128)(2,1)} %param.4), channel_id=1, source_target_pairs={{0,2},{2,4},{4,6},{6,8},{8,10},{10,12},{12,14},{14,0},{1,3},{3,5},... | collective-permute-start | bytes 786440 | tf_op jit(solution)/shard_map/ppermute | solution.py:20
  0.7 20.2 %collective-permute-start.4 = (bf16[1,2,8,16,512]{4,3,2,1,0:T(8,128)(2,1)}, bf16[1,2,8,16,512]{4,3,2,1,0:T(8,128)(2,1)S(1)}, u32[]{:S(2)}, u32[]{:S(2)}) collective-permute-start(bf16[1,2,8,16,512]{4,3,2,1,0:T(8,128)(2,1)} %param.4), channel_id=1, source_target_pairs={{0,14},{2,0},{4,2},{6,4},{8,6},{10,8},{12,10},{14,12},{1,15},{3,1}... | collective-permute-start | bytes 786440 | tf_op jit(solution)/shard_map/ppermute | solution.py:22
  3.4 6.7 %collective-permute-start.9 = (bf16[1,1,8,16,512]{4,3,2,1,0:T(8,128)(2,1)S(1)}, bf16[1,1,8,16,512]{4,3,2,1,0:T(8,128)(2,1)S(1)}, u32[]{:S(2)}, u32[]{:S(2)}) collective-permute-start(bf16[1,1,8,16,512]{4,3,2,1,0:T(8,128)(2,1)S(1)} %get-tuple-element.31), channel_id=1, source_target_pairs={{0,16},{16,32},{32,48},{48,64},{64,80},{80,96},{96,112},{112,128},... | collective-permute-start | bytes 393224 | tf_op jit(solution)/shard_map/ppermute | solution.py:35
  7.2 7.1 %collective-permute-start.10 = (bf16[1,1,8,16,512]{4,3,2,1,0:T(8,128)(2,1)S(1)}, bf16[1,1,8,16,512]{4,3,2,1,0:T(8,128)(2,1)S(1)}, u32[]{:S(2)}, u32[]{:S(2)}) collective-permute-start(bf16[1,1,8,16,512]{4,3,2,1,0:T(8,128)(2,1)S(1)} %get-tuple-element.30), channel_id=1, source_target_pairs={{16,0},{32,16},{48,32},{64,48},{80,64},{96,80},{112,96},{128,112},... | collective-permute-start | bytes 393224 | tf_op jit(solution)/shard_map/ppermute | solution.py:35
  14.7 5.8 %collective-permute-start.1 = (bf16[1,2,8,16,512]{4,3,2,1,0:T(8,128)(2,1)S(1)}, bf16[1,2,8,16,512]{4,3,2,1,0:T(8,128)(2,1)S(1)}, u32[]{:S(2)}, u32[]{:S(2)}) collective-permute-start(bf16[1,2,8,16,512]{4,3,2,1,0:T(8,128)(2,1)S(1)} %collective-permute-done), channel_id=1, source_target_pairs={{0,2},{2,4},{4,6},{6,8},{8,10},{10,12},{12,14},{14,0},{1,3},{3,5},... | collective-permute-start | bytes 786440 | tf_op jit(solution)/shard_map/ppermute | solution.py:20
  14.9 17.2 %copy-start.1 = (bf16[1,2,8,16,512]{4,3,2,1,0:T(8,128)(2,1)S(1)}, bf16[1,2,8,16,512]{4,3,2,1,0:T(8,128)(2,1)}, u32[]{:S(2)}) copy-start(bf16[1,2,8,16,512]{4,3,2,1,0:T(8,128)(2,1)} %param.4) | copy-start | bytes 786436
  20.5 5.8 %collective-permute-start.2 = (bf16[1,2,8,16,512]{4,3,2,1,0:T(8,128)(2,1)S(1)}, bf16[1,2,8,16,512]{4,3,2,1,0:T(8,128)(2,1)S(1)}, u32[]{:S(2)}, u32[]{:S(2)}) collective-permute-start(bf16[1,2,8,16,512]{4,3,2,1,0:T(8,128)(2,1)S(1)} %collective-permute-done.1), channel_id=1, source_target_pairs={{0,2},{2,4},{4,6},{6,8},{8,10},{10,12},{12,14},{14,0},{1,3},{3,5},... | collective-permute-start | bytes 786440 | tf_op jit(solution)/shard_map/ppermute | solution.py:20
  20.8 6.0 %collective-permute-start.5 = (bf16[1,2,8,16,512]{4,3,2,1,0:T(8,128)(2,1)S(1)}, bf16[1,2,8,16,512]{4,3,2,1,0:T(8,128)(2,1)S(1)}, u32[]{:S(2)}, u32[]{:S(2)}) collective-permute-start(bf16[1,2,8,16,512]{4,3,2,1,0:T(8,128)(2,1)S(1)} %collective-permute-done.4), channel_id=1, source_target_pairs={{0,14},{2,0},{4,2},{6,4},{8,6},{10,8},{12,10},{14,12},{1,15},{3,1}... | collective-permute-start | bytes 786440 | tf_op jit(solution)/shard_map/ppermute | solution.py:22
  26.3 5.8 %collective-permute-start.3 = (bf16[1,2,8,16,512]{4,3,2,1,0:T(8,128)(2,1)S(1)}, bf16[1,2,8,16,512]{4,3,2,1,0:T(8,128)(2,1)S(1)}, u32[]{:S(2)}, u32[]{:S(2)}) collective-permute-start(bf16[1,2,8,16,512]{4,3,2,1,0:T(8,128)(2,1)S(1)} %collective-permute-done.2), channel_id=1, source_target_pairs={{0,2},{2,4},{4,6},{6,8},{8,10},{10,12},{12,14},{14,0},{1,3},{3,5},... | collective-permute-start | bytes 786440 | tf_op jit(solution)/shard_map/ppermute | solution.py:20
  26.8 5.8 %collective-permute-start.6 = (bf16[1,2,8,16,512]{4,3,2,1,0:T(8,128)(2,1)S(1)}, bf16[1,2,8,16,512]{4,3,2,1,0:T(8,128)(2,1)S(1)}, u32[]{:S(2)}, u32[]{:S(2)}) collective-permute-start(bf16[1,2,8,16,512]{4,3,2,1,0:T(8,128)(2,1)S(1)} %collective-permute-done.5), channel_id=1, source_target_pairs={{0,14},{2,0},{4,2},{6,4},{8,6},{10,8},{12,10},{14,12},{1,15},{3,1}... | collective-permute-start | bytes 786440 | tf_op jit(solution)/shard_map/ppermute | solution.py:22
  35.2 13.1 %collective-permute-start.11 = (f32[27,16,128]{2,1,0:T(8,128)S(1)}, f32[27,16,128]{2,1,0:T(8,128)S(1)}, u32[]{:S(2)}, u32[]{:S(2)}) collective-permute-start(f32[27,16,128]{2,1,0:T(8,128)S(1)} %bitcast.185), channel_id=1, source_target_pairs={{0,1},{1,0},{2,3},{3,2},{4,5},{5,4},{6,7},{7,6},{8,9},{9,8},{10,11... | collective-permute-start | bytes 663560 | tf_op jit(solution)/shard_map/ppermute | solution.py:40
  39.6 49.5 %collective-permute-start.8 = (f32[1,1,8,16,512]{4,3,2,1,0:T(8,128)S(1)}, f32[1,1,8,16,512]{4,3,2,1,0:T(8,128)S(1)}, u32[]{:S(2)}, u32[]{:S(2)}) collective-permute-start(f32[1,1,8,16,512]{4,3,2,1,0:T(8,128)S(1)} %get-tuple-element.27), channel_id=1, source_target_pairs={{16,0},{32,16},{48,32},{64,48},{80,64},{96,80},{112,96},{128,112},... | collective-permute-start | bytes 786440 | tf_op jit(solution)/shard_map/ppermute | solution.py:35
  43.7 45.4 %collective-permute-start.7 = (f32[1,1,8,16,512]{4,3,2,1,0:T(8,128)S(1)}, f32[1,1,8,16,512]{4,3,2,1,0:T(8,128)S(1)}, u32[]{:S(2)}, u32[]{:S(2)}) collective-permute-start(f32[1,1,8,16,512]{4,3,2,1,0:T(8,128)S(1)} %get-tuple-element.28), channel_id=1, source_target_pairs={{0,16},{16,32},{32,48},{48,64},{64,80},{80,96},{96,112},{112,128},... | collective-permute-start | bytes 786440 | tf_op jit(solution)/shard_map/ppermute | solution.py:35
  48.3 11.3 %collective-permute-start.12 = (f32[27,16,128]{2,1,0:T(8,128)S(1)}, f32[27,16,128]{2,1,0:T(8,128)S(1)}, u32[]{:S(2)}, u32[]{:S(2)}) collective-permute-start(f32[27,16,128]{2,1,0:T(8,128)S(1)} %add.196), channel_id=1, source_target_pairs={{0,16},{16,0},{32,48},{48,32},{64,80},{80,64},{96,112},{112,96},{1... | collective-permute-start | bytes 663560 | tf_op jit(solution)/shard_map/ppermute | solution.py:40
  59.6 14.5 %collective-permute-start.13 = (f32[27,16,128]{2,1,0:T(8,128)S(1)}, f32[27,16,128]{2,1,0:T(8,128)S(1)}, u32[]{:S(2)}, u32[]{:S(2)}) collective-permute-start(f32[27,16,128]{2,1,0:T(8,128)S(1)} %add.197), channel_id=1, source_target_pairs={{0,128},{16,144},{32,160},{48,176},{64,192},{80,208},{96,224},{112... | collective-permute-start | bytes 663560 | tf_op jit(solution)/shard_map/ppermute | solution.py:40
  74.1 12.8 %collective-permute-start.14 = (f32[27,16,128]{2,1,0:T(8,128)S(1)}, f32[27,16,128]{2,1,0:T(8,128)S(1)}, u32[]{:S(2)}, u32[]{:S(2)}) collective-permute-start(f32[27,16,128]{2,1,0:T(8,128)S(1)} %add.198), channel_id=1, source_target_pairs={{0,32},{16,48},{32,0},{48,16},{64,96},{80,112},{96,64},{112,80},{1... | collective-permute-start | bytes 663560 | tf_op jit(solution)/shard_map/ppermute | solution.py:40
  87.0 13.5 %collective-permute-start.15 = (f32[27,16,128]{2,1,0:T(8,128)S(1)}, f32[27,16,128]{2,1,0:T(8,128)S(1)}, u32[]{:S(2)}, u32[]{:S(2)}) collective-permute-start(f32[27,16,128]{2,1,0:T(8,128)S(1)} %add.199), channel_id=1, source_target_pairs={{0,64},{16,80},{32,96},{48,112},{64,0},{80,16},{96,32},{112,48},{1... | collective-permute-start | bytes 663560 | tf_op jit(solution)/shard_map/ppermute | solution.py:40
